TPU v7x, 32 devices: a whole 2x2x4 slice. The times are simulated.
32 devices in a mesh: row: 8 (over z, y), col: 4 (over x, core).
Axes of the slice: x: 2, y: 2, z: 4, core: 2. Of those that a mesh axis runs over, the one named last changes fastest.
Arguments:
- gram: float32 [16384, 16384], P('row', 'col'), may hold values from -1 to 17, as said below
Outputs:
- factored: float32 [16384, 16384], P('row', 'col')
Inputs may be any that keep to these rules, and one draw needn't show every extreme that they name: gram holds a symmetric positive definite matrix in the block-cyclic order of the steps.
All inputs are finite; a program needn't handle non-finite values.
Results may differ from a plain program's by a relative error of at most 0.0001.
Values sent between devices are 32-bit elements; how exact they have to be, the bound alone decides.
No kernel may reach another device: no remote copies, remote signals or barrier semaphores. Data moves between devices by JAX's collectives and lax.ppermute only.
A program may use at most 192 MiB of HBM per device.

v0:
```python
import jax
import jax.numpy as jnp
from jax import lax
from jax.sharding import PartitionSpec as P

NB = 512
STEPS = 2


def broadcast(value, axis, source):
    kept = jnp.where(lax.axis_index(axis) == source, value, 0).astype(value.dtype)
    return lax.psum(kept, axis)


def from_partner(block, axis, apart):
    count = lax.axis_size(axis)
    route = []
    for low in range(count):
        high = low | 1 << apart
        if high != low and high < count:
            route += [(low, high), (high, low)]
    return lax.ppermute(block, axis, route)


def global_index(count, block, grid, position):
    ladder = jnp.arange(count, dtype=jnp.int32)
    return (ladder // block * grid + position) * block + ladder % block


def times_transposed(left, right):
    return lax.dot_general(
        left,
        right,
        (((1,), (1,)), ((), ())),
        precision=lax.Precision.HIGHEST,
        preferred_element_type=jnp.float32,
    )


def local(gram):
    grid_rows = lax.axis_size("row")
    grid_cols = lax.axis_size("col")
    row_id = lax.axis_index("row")
    col_id = lax.axis_index("col")
    rblock = NB * grid_cols // grid_rows
    per_class = grid_rows // grid_cols
    local_rows = gram.shape[0]
    local_cols = gram.shape[1]
    blocks = local_rows // rblock
    grows = global_index(local_rows, rblock, grid_rows, row_id)
    gcols = global_index(local_cols, NB, grid_cols, col_id)
    member = row_id % per_class
    row_class = row_id // per_class
    identity = jnp.eye(NB, dtype=jnp.float32)

    def factor_panel(matrix, panel_index):
        owner_col = panel_index % grid_cols
        local_block = panel_index // grid_cols
        end_row = panel_index * NB + NB
        column = matrix[:, local_block * NB : (local_block + 1) * NB]
        square = column[local_block * rblock : (local_block + 1) * rblock]
        is_owner = col_id == owner_col
        in_class = row_class == owner_col
        select = (jnp.arange(per_class, dtype=jnp.int32) == member).astype(jnp.float32)
        weight = jnp.where(is_owner & in_class, 1.0, 0.0).astype(jnp.float32)
        placed = (select[:, None, None] * square[None]).reshape(NB, NB) * weight
        diagonal = lax.psum(placed, "row")
        diagonal = jnp.where(is_owner, diagonal, identity)
        low_factor = jnp.linalg.cholesky(diagonal)
        inverse = jax.scipy.linalg.solve_triangular(low_factor, identity, lower=True)
        solved = times_transposed(column, inverse)
        trailing = jnp.where((grows >= end_row)[:, None], solved, 0.0)
        rows_diag = lax.dynamic_slice_in_dim(low_factor, member * rblock, rblock, 0)
        previous = trailing[local_block * rblock : (local_block + 1) * rblock]
        patched = jnp.where(in_class, rows_diag, previous)
        factored = trailing.at[local_block * rblock : (local_block + 1) * rblock].set(patched)
        new_column = jnp.where(is_owner, factored, column)
        matrix = matrix.at[:, local_block * NB : (local_block + 1) * NB].set(new_column)
        return (matrix, trailing)

    matrix = gram
    for panel_index in range(STEPS):
        matrix, trailing = factor_panel(matrix, panel_index)
        spread_owner_col = panel_index % grid_cols
        spread_rows_all = broadcast(trailing, "col", spread_owner_col)
        pieces = spread_rows_all.reshape(grid_cols, blocks // grid_cols * rblock, NB)
        shift_bits = per_class.bit_length() - 1
        for bit_level in reversed(range(grid_cols.bit_length() - 1)):
            halfway = pieces.shape[0] // 2
            own_bit = row_class >> bit_level & 1
            wanted = col_id >> bit_level & 1
            upper = own_bit == 1
            retained = jnp.where(upper, pieces[halfway:], pieces[:halfway])
            outgoing = jnp.where(upper, pieces[:halfway], pieces[halfway:])
            received = from_partner(outgoing, "row", shift_bits + bit_level)
            pieces = jnp.where(own_bit == wanted, retained, received)
        gathered = lax.all_gather(pieces[0], "row", axis=0, tiled=True)
        spread_columns = gathered.reshape(grid_cols, per_class, blocks // grid_cols, rblock, NB)
        spread_columns = jnp.transpose(spread_columns, (0, 2, 1, 3, 4)).reshape(local_cols, NB)
        first_row = panel_index * NB
        apply_end_row = first_row + NB
        current = matrix
        updated = current - times_transposed(spread_rows_all, spread_columns)
        panel_rows = (grows >= first_row) & (grows < apply_end_row)
        beyond = gcols >= apply_end_row
        updated = jnp.where(panel_rows[:, None] & beyond[None, :], 0.0, updated)
        matrix = matrix.at[:, 0:local_cols].set(updated)
    matrix, trailing = factor_panel(matrix, STEPS)
    return matrix


def solution(mesh):
    placed = (P("row", "col"),)
    return jax.shard_map(
        local, mesh=mesh, in_specs=placed, out_specs=P("row", "col"), check_vma=False
    )
```

profile of v0, /device:TPU:0, one launch (start us, length us, event | category | flops | bytes accessed | tf_op | source)
XLA Modules:
  0.0 1543.9 jit_solution(489001765417519902)
XLA Ops:
  6.5 23.0 %copy.106 = f32[2048,4096]{1,0:T(8,128)} copy(f32[2048,4096]{1,0:T(8,128)} %param.24) | data formatting | bytes 67108864
  32.8 81.1 %all-reduce.7.cloned.1.call-done = f32[512,512]{0,1:T(8,128)} async-done(((f32[512,512]{0,1:T(8,128)}), f32[512,512]{0,1:T(8,128)}) %all-reduce.7.cloned.1.call-update) | async-done | bytes 1048592 | tf_op jit(solution)/shard_map/psum | solution.py:67
  185.1 11.7 cholesky.431
  211.4 39.3 %custom-call.34 = f32[4,128,128]{1,2,0:T(8,128)S(1)} custom-call(f32[4,128,128]{2,1,0:T(8,128)S(1)} %get-tuple-element.139), custom_call_target="InvertDiagBlocksLowerTriangular" | custom-call | tf_op jit(solution)/shard_map/jit(_solve_triangular)/triangular_solve | solution.py:70
  266.2 84.3 %all-reduce.9.cloned.1.call-done = f32[2048,512]{1,0:T(8,128)} async-done(((f32[2048,512]{1,0:T(8,128)}), f32[2048,512]{1,0:T(8,128)}) %all-reduce.9.cloned.1.call-update) | async-done | bytes 4194320 | tf_op jit(solution)/shard_map/psum | solution.py:12
  357.7 90.7 %collective-permute-done = f32[2,512,512]{2,1,0:T(8,128)S(1)} collective-permute-done((f32[2,512,512]{2,1,0:T(8,128)}, f32[2,512,512]{2,1,0:T(8,128)S(1)}, u32[]{:S(2)}, u32[]{:S(2)}) %collective-permute-start) | collective-permute-done | bytes 2097184 | tf_op jit(solution)/shard_map/ppermute | solution.py:22
  453.6 23.9 %collective-permute-done.1 = f32[1,512,512]{2,1,0:T(8,128)} collective-permute-done((f32[1,512,512]{2,1,0:T(8,128)}, f32[1,512,512]{2,1,0:T(8,128)}, u32[]{:S(2)}, u32[]{:S(2)}) %collective-permute-start.1) | collective-permute-done | bytes 1048608 | tf_op jit(solution)/shard_map/ppermute | solution.py:22
  489.3 116.8 %all-gather.5.cloned.1.call-done = f32[1,4096,512]{2,1,0:T(8,128)} async-done(((f32[1,512,512]{2,1,0:T(8,128)}), f32[1,4096,512]{2,1,0:T(8,128)}) %all-gather.5.cloned.1.call-update) | async-done | bytes 8388624 | tf_op jit(solution)/shard_map/all_gather | solution.py:97
  610.7 60.7 %subtract_select_fusion.1 = f32[2048,4096]{1,0:T(8,128)} fusion(f32[2048,4096]{1,0:T(8,128)} %fusion, pred[4096]{0:T(1024)(128)(4,1)S(1)} %broadcast_compare_fusion.1, pred[2048]{0:T(1024)(128)(4,1)S(1)} %get-tuple-element.222, f32[2048,512]{1,0:T(8,128)S(1)} %copy-done, f32[4096,512]{1,0:T(8,128)S(1)} %bitcast.177), kind=kOutput, calls=%fused_computation.7 | convolution fusion | flops 51564773376 | bytes 79697920 | tf_op jit(solution)/shard_map/dot_general | solution.py:31
  674.6 76.4 %all-reduce.11.cloned.1.call-done = f32[512,512]{0,1:T(8,128)} async-done(((f32[512,512]{0,1:T(8,128)}), f32[512,512]{0,1:T(8,128)}) %all-reduce.11.cloned.1.call-update) | async-done | bytes 1048592 | tf_op jit(solution)/shard_map/psum | solution.py:67
  776.4 11.7 cholesky.465
  798.8 11.7 cholesky.486
  821.0 11.7 cholesky.503
  848.2 39.3 %custom-call.38 = f32[4,128,128]{1,2,0:T(8,128)S(1)} custom-call(f32[4,128,128]{2,1,0:T(8,128)S(1)} %get-tuple-element.140), custom_call_target="InvertDiagBlocksLowerTriangular" | custom-call | tf_op jit(solution)/shard_map/jit(_solve_triangular)/triangular_solve | solution.py:70
  903.1 85.0 %all-reduce.13.cloned.1.call-done = f32[2048,512]{1,0:T(8,128)} async-done(((f32[2048,512]{1,0:T(8,128)}), f32[2048,512]{1,0:T(8,128)}) %all-reduce.13.cloned.1.call-update) | async-done | bytes 4194320 | tf_op jit(solution)/shard_map/psum | solution.py:12
  993.4 90.5 %collective-permute-done.2 = f32[2,512,512]{2,1,0:T(8,128)S(1)} collective-permute-done((f32[2,512,512]{2,1,0:T(8,128)S(1)}, f32[2,512,512]{2,1,0:T(8,128)S(1)}, u32[]{:S(2)}, u32[]{:S(2)}) %collective-permute-start.2) | collective-permute-done | bytes 2097184 | tf_op jit(solution)/shard_map/ppermute | solution.py:22
  1085.1 23.7 %collective-permute-done.3 = f32[1,512,512]{2,1,0:T(8,128)S(1)} collective-permute-done((f32[1,512,512]{2,1,0:T(8,128)S(1)}, f32[1,512,512]{2,1,0:T(8,128)S(1)}, u32[]{:S(2)}, u32[]{:S(2)}) %collective-permute-start.3) | collective-permute-done | bytes 1048608 | tf_op jit(solution)/shard_map/ppermute | solution.py:22
  1118.1 118.1 %all-gather.7.cloned.1.call-done = f32[1,4096,512]{2,1,0:T(8,128)} async-done(((f32[1,512,512]{2,1,0:T(8,128)}), f32[1,4096,512]{2,1,0:T(8,128)}) %all-gather.7.cloned.1.call-update) | async-done | bytes 8388624 | tf_op jit(solution)/shard_map/all_gather | solution.py:97
  1240.8 60.9 %subtract_select_fusion = f32[2048,4096]{1,0:T(8,128)} fusion(f32[2048,4096]{1,0:T(8,128)} %fusion.1, pred[4096]{0:T(1024)(128)(4,1)S(1)} %broadcast_compare_fusion, pred[2048]{0:T(1024)(128)(4,1)S(1)} %compare_and_fusion.1, f32[2048,512]{1,0:T(8,128)S(1)} %copy-done.1, f32[4096,512]{1,0:T(8,128)S(1)} %bitcast.178), kind=kOutput, calls=%fused_computation.6 | convolution fusion | flops 51564773376 | bytes 79697920 | tf_op jit(solution)/shard_map/dot_general | solution.py:31
  1304.6 76.6 %all-reduce.15.cloned.1.call-done = f32[512,512]{0,1:T(8,128)} async-done(((f32[512,512]{0,1:T(8,128)}), f32[512,512]{0,1:T(8,128)}) %all-reduce.15.cloned.1.call-update) | async-done | bytes 1048592 | tf_op jit(solution)/shard_map/psum | solution.py:67
  1406.6 11.7 cholesky.537
  1429.3 11.7 cholesky.558
  1451.4 11.9 cholesky.575
  1478.0 39.3 %custom-call.42 = f32[4,128,128]{1,2,0:T(8,128)S(1)} custom-call(f32[4,128,128]{2,1,0:T(8,128)S(1)} %get-tuple-element.141), custom_call_target="InvertDiagBlocksLowerTriangular" | custom-call | tf_op jit(solution)/shard_map/jit(_solve_triangular)/triangular_solve | solution.py:70
  (223 shorter events, 334.4 us)
Async XLA Ops:
  6.5 107.3 %all-reduce.7.cloned.1.call-start = ((), (), s32[]{:S(2)}) async-start(), calls=%async_computation | async-start | bytes 2097152 | tf_op jit(solution)/shard_map/psum | solution.py:67
  32.6 317.9 %all-reduce.9.cloned.1.call-start = ((), (), s32[]{:S(2)}) async-start(), calls=%async_computation.1 | async-start | bytes 8388608 | tf_op jit(solution)/shard_map/psum | solution.py:12
  113.9 2.8 copy-start.2
  266.2 340.0 %all-gather.5.cloned.1.call-start = ((), (), s32[]{:S(2)}) async-start(), calls=%async_computation.5 | async-start | bytes 9437184 | tf_op jit(solution)/shard_map/all_gather | solution.py:97
  355.3 93.1 %collective-permute-start = (f32[2,512,512]{2,1,0:T(8,128)}, f32[2,512,512]{2,1,0:T(8,128)S(1)}, u32[]{:S(2)}, u32[]{:S(2)}) collective-permute-start(f32[2,512,512]{2,1,0:T(8,128)} %bitcast.13), channel_id=1, source_target_pairs={{0,16},{16,0},{4,20},{20,4},{8,24},{24,8},{12,28},{28,12},{1,17},{... | collective-permute-start | bytes 6291464 | tf_op jit(solution)/shard_map/ppermute | solution.py:22
  448.4 1.3 copy-start.7
  453.0 24.5 %collective-permute-start.1 = (f32[1,512,512]{2,1,0:T(8,128)}, f32[1,512,512]{2,1,0:T(8,128)}, u32[]{:S(2)}, u32[]{:S(2)}) collective-permute-start(f32[1,512,512]{2,1,0:T(8,128)} %slice_select_fusion.5), channel_id=1, source_target_pairs={{0,8},{8,0},{4,12},{12,4},{16,24},{24,16},{20,28},{28,20},{1,9},{9... | collective-permute-start | bytes 3145736 | tf_op jit(solution)/shard_map/ppermute | solution.py:22
  478.9 272.1 %all-reduce.11.cloned.1.call-start = ((), (), s32[]{:S(2)}) async-start(), calls=%async_computation.2 | async-start | bytes 2097152 | tf_op jit(solution)/shard_map/psum | solution.py:67
  606.1 4.6 copy-start
  674.4 313.7 %all-reduce.13.cloned.1.call-start = ((), (), s32[]{:S(2)}) async-start(), calls=%async_computation.3 | async-start | bytes 8388608 | tf_op jit(solution)/shard_map/psum | solution.py:12
  751.0 1.5 copy-start.3
  902.9 333.3 %all-gather.7.cloned.1.call-start = ((), (), s32[]{:S(2)}) async-start(), calls=%async_computation.6 | async-start | bytes 9437184 | tf_op jit(solution)/shard_map/all_gather | solution.py:97
  990.9 93.0 %collective-permute-start.2 = (f32[2,512,512]{2,1,0:T(8,128)S(1)}, f32[2,512,512]{2,1,0:T(8,128)S(1)}, u32[]{:S(2)}, u32[]{:S(2)}) collective-permute-start(f32[2,512,512]{2,1,0:T(8,128)S(1)} %bitcast.189), channel_id=1, source_target_pairs={{0,16},{16,0},{4,20},{20,4},{8,24},{24,8},{12,28},{28,12},{1,17},{... | collective-permute-start | bytes 6291464 | tf_op jit(solution)/shard_map/ppermute | solution.py:22
  1084.3 26.0 %copy-start.5 = (f32[512,512]{1,0:T(8,128)S(1)}, f32[512,512]{1,0:T(8,128)}, u32[]{:S(2)}) copy-start(f32[512,512]{1,0:T(8,128)} %get-tuple-element.169) | copy-start | bytes 3145732
  1084.6 24.2 %collective-permute-start.3 = (f32[1,512,512]{2,1,0:T(8,128)S(1)}, f32[1,512,512]{2,1,0:T(8,128)S(1)}, u32[]{:S(2)}, u32[]{:S(2)}) collective-permute-start(f32[1,512,512]{2,1,0:T(8,128)S(1)} %slice_select_fusion.4), channel_id=1, source_target_pairs={{0,8},{8,0},{4,12},{12,4},{16,24},{24,16},{20,28},{28,20},{1,9},{9... | collective-permute-start | bytes 3145736 | tf_op jit(solution)/shard_map/ppermute | solution.py:22
  1110.2 271.1 %all-reduce.15.cloned.1.call-start = ((), (), s32[]{:S(2)}) async-start(), calls=%async_computation.4 | async-start | bytes 2097152 | tf_op jit(solution)/shard_map/psum | solution.py:67
  1236.2 4.6 copy-start.1
  1381.3 1.5 copy-start.4
  1522.1 8.7 copy-start.6
Sparse Core Ops, SparseCore 0:
  32.7 81.0 all-reduce.6
  266.3 84.1 all-reduce.8
  479.1 127.0 all-gather.4
  674.5 76.4 all-reduce.10
  903.0 85.0 all-reduce.12
  1110.3 125.8 all-gather.6
  1304.7 76.4 all-reduce.14
where the time goes:
time: 1550 us; the launch traced here: 1540 us
  waiting for transfers between devices  867 us (56%)
  other arithmetic  408 us (26%)
  matrix products  171 us (11%)
  local copies, waits for them, and re-layouts  67.9 us (4%)
  between operations  22.3 us (1%)
    another operation x44, other arithmetic, factor_panel(): low_factor = jnp.linalg.cholesky(diagonal)  238 us
    all_gather x2, waiting for transfers between devices, local(): gathered = lax.all_gather(pieces[0], 'row', axis=0, tiled=True)  235 us
    psum x3, waiting for transfers between devices, factor_panel(): diagonal = lax.psum(placed, 'row')  234 us
    ppermute x4, waiting for transfers between devices, from_partner(): return lax.ppermute(block, axis, route)  229 us
    psum x2, waiting for transfers between devices, broadcast(): return lax.psum(kept, axis)  169 us
    dot_general x5, matrix products, times_transposed(): lax.dot_general(left, right, (((1,), (1,)), ((), ())), precision=lax.Prec...  152 us
    another operation x7, other arithmetic, factor_panel(): jax.scipy.linalg.solve_triangular(low_factor, identity, lower=True)  122 us
  transfers between devices with their start and end apart: 11, of which 11 were waited for; matrix products, arithmetic and copies ran while one was open for 1% of the time, Pallas kernels for 0%

commit v1 on v0

--- a/solution.py
+++ b/solution.py
@@ -2,6 +2,7 @@
 import jax.numpy as jnp
 from jax import lax
 from jax.sharding import PartitionSpec as P
+from jax.lax import axis_size, ppermute
 
 NB = 512
 STEPS = 2
@@ -64,7 +65,15 @@
         select = (jnp.arange(per_class, dtype=jnp.int32) == member).astype(jnp.float32)
         weight = jnp.where(is_owner & in_class, 1.0, 0.0).astype(jnp.float32)
         placed = (select[:, None, None] * square[None]).reshape(NB, NB) * weight
-        diagonal = lax.psum(placed, "row")
+        diagonal, tmp = (placed, 0)
+        ndev = axis_size("row")
+        while 1 << tmp < ndev:
+            gallery = []
+            for no in tuple(range(ndev)):
+                gallery.append((no, no ^ 1 << tmp))
+            e_next = ppermute(diagonal, axis_name="row", perm=gallery)
+            diagonal = diagonal + e_next
+            tmp = tmp + 1
         diagonal = jnp.where(is_owner, diagonal, identity)
         low_factor = jnp.linalg.cholesky(diagonal)
         inverse = jax.scipy.linalg.solve_triangular(low_factor, identity, lower=True)

time: 1550 us -> 1610 us (1.039)
  waiting for transfers between devices: 867 us -> 907 us
    ppermute x0 -> x9, waiting for transfers between devices: none -> 272 us  [factor_panel(): e_next = ppermute(diagonal, axis_name='row', perm=gallery)]
    psum x3 -> x0, waiting for transfers between devices: 234 us -> none  [factor_panel(): diagonal = lax.psum(placed, 'row')]
  transfers between devices with their start and end apart: 11 -> 17, of which waited for: 11 -> 17; matrix products, arithmetic and copies ran while one was open for 1% -> 1% of each run, Pallas kernels for 0% -> 0%
where the time goes in v1:
time: 1610 us; the launch traced here: 1600 us
  waiting for transfers between devices  907 us (56%)
  other arithmetic  404 us (25%)
  matrix products  182 us (11%)
  local copies, waits for them, and re-layouts  67.7 us (4%)
  between operations  22.1 us (1%)
  starting transfers between devices  18.9 us (1%)
    ppermute x9, waiting for transfers between devices, factor_panel(): e_next = ppermute(diagonal, axis_name='row', perm=gallery)  272 us
    another operation x44, other arithmetic, factor_panel(): low_factor = jnp.linalg.cholesky(diagonal)  238 us
    all_gather x2, waiting for transfers between devices, local(): gathered = lax.all_gather(pieces[0], 'row', axis=0, tiled=True)  235 us
    ppermute x4, waiting for transfers between devices, from_partner(): return lax.ppermute(block, axis, route)  229 us
    psum x2, waiting for transfers between devices, broadcast(): return lax.psum(kept, axis)  172 us
    dot_general x5, matrix products, times_transposed(): lax.dot_general(left, right, (((1,), (1,)), ((), ())), precision=lax.Prec...  152 us
    another operation x7, other arithmetic, factor_panel(): jax.scipy.linalg.solve_triangular(low_factor, identity, lower=True)  122 us
  transfers between devices with their start and end apart: 17, of which 17 were waited for; matrix products, arithmetic and copies ran while one was open for 1% of the time, Pallas kernels for 0%

profile of v1, /device:TPU:0, one launch (start us, length us, event | category | flops | bytes accessed | tf_op | source)
XLA Modules:
  0.0 1603.1 jit_solution(9918298096184406419)
XLA Ops:
  6.5 23.0 %copy.103 = f32[2048,4096]{1,0:T(8,128)} copy(f32[2048,4096]{1,0:T(8,128)} %param.24) | data formatting | bytes 67108864
  34.6 23.2 %collective-permute-done = f32[512,512]{0,1:T(8,128)S(1)} collective-permute-done((f32[512,512]{0,1:T(8,128)S(1)}, f32[512,512]{0,1:T(8,128)S(1)}, u32[]{:S(2)}, u32[]{:S(2)}) %collective-permute-start) | collective-permute-done | bytes 1048608 | tf_op jit(solution)/shard_map/ppermute | solution.py:74
  59.9 22.5 %collective-permute-done.1 = f32[512,512]{0,1:T(8,128)S(1)} collective-permute-done((f32[512,512]{0,1:T(8,128)S(1)}, f32[512,512]{0,1:T(8,128)S(1)}, u32[]{:S(2)}, u32[]{:S(2)}) %collective-permute-start.1) | collective-permute-done | bytes 1048608 | tf_op jit(solution)/shard_map/ppermute | solution.py:74
  85.3 44.3 %collective-permute-done.2 = f32[512,512]{0,1:T(8,128)} collective-permute-done((f32[512,512]{0,1:T(8,128)S(1)}, f32[512,512]{0,1:T(8,128)}, u32[]{:S(2)}, u32[]{:S(2)}) %collective-permute-start.2) | collective-permute-done | bytes 1048608 | tf_op jit(solution)/shard_map/ppermute | solution.py:74
  229.5 39.3 %custom-call.34 = f32[4,128,128]{1,2,0:T(8,128)S(1)} custom-call(f32[4,128,128]{2,1,0:T(8,128)S(1)} %get-tuple-element.139), custom_call_target="InvertDiagBlocksLowerTriangular" | custom-call | tf_op jit(solution)/shard_map/jit(_solve_triangular)/triangular_solve | solution.py:79
  284.3 86.4 %all-reduce.4.cloned.1.call-done = f32[2048,512]{1,0:T(8,128)} async-done(((f32[2048,512]{1,0:T(8,128)}), f32[2048,512]{1,0:T(8,128)}) %all-reduce.4.cloned.1.call-update) | async-done | bytes 4194320 | tf_op jit(solution)/shard_map/psum | solution.py:13
  377.9 90.7 %collective-permute-done.3 = f32[2,512,512]{2,1,0:T(8,128)S(1)} collective-permute-done((f32[2,512,512]{2,1,0:T(8,128)}, f32[2,512,512]{2,1,0:T(8,128)S(1)}, u32[]{:S(2)}, u32[]{:S(2)}) %collective-permute-start.3) | collective-permute-done | bytes 2097184 | tf_op jit(solution)/shard_map/ppermute | solution.py:23
  473.8 23.9 %collective-permute-done.4 = f32[1,512,512]{2,1,0:T(8,128)} collective-permute-done((f32[1,512,512]{2,1,0:T(8,128)}, f32[1,512,512]{2,1,0:T(8,128)}, u32[]{:S(2)}, u32[]{:S(2)}) %collective-permute-start.4) | collective-permute-done | bytes 1048608 | tf_op jit(solution)/shard_map/ppermute | solution.py:23
  509.5 116.8 %all-gather.5.cloned.1.call-done = f32[1,4096,512]{2,1,0:T(8,128)} async-done(((f32[1,512,512]{2,1,0:T(8,128)}), f32[1,4096,512]{2,1,0:T(8,128)}) %all-gather.5.cloned.1.call-update) | async-done | bytes 8388624 | tf_op jit(solution)/shard_map/all_gather | solution.py:106
  630.9 60.9 %subtract_select_fusion.1 = f32[2048,4096]{1,0:T(8,128)} fusion(f32[2048,4096]{1,0:T(8,128)} %fusion, pred[4096]{0:T(1024)(128)(4,1)S(1)} %broadcast_compare_fusion.1, pred[2048]{0:T(1024)(128)(4,1)S(1)} %get-tuple-element.222, f32[2048,512]{1,0:T(8,128)S(1)} %copy-done, f32[4096,512]{1,0:T(8,128)S(1)} %bitcast.177), kind=kOutput, calls=%fused_computation.7 | convolution fusion | flops 51564773376 | bytes 79697920 | tf_op jit(solution)/shard_map/dot_general | solution.py:32
  694.3 23.6 %collective-permute-done.5 = f32[512,512]{0,1:T(8,128)S(1)} collective-permute-done((f32[512,512]{0,1:T(8,128)S(1)}, f32[512,512]{0,1:T(8,128)S(1)}, u32[]{:S(2)}, u32[]{:S(2)}) %collective-permute-start.5) | collective-permute-done | bytes 1048608 | tf_op jit(solution)/shard_map/ppermute | solution.py:74
  718.3 23.3 %collective-permute-done.6 = f32[512,512]{0,1:T(8,128)S(1)} collective-permute-done((f32[512,512]{0,1:T(8,128)S(1)}, f32[512,512]{0,1:T(8,128)S(1)}, u32[]{:S(2)}, u32[]{:S(2)}) %collective-permute-start.6) | collective-permute-done | bytes 1048608 | tf_op jit(solution)/shard_map/ppermute | solution.py:74
  743.7 44.1 %collective-permute-done.7 = f32[512,512]{0,1:T(8,128)} collective-permute-done((f32[512,512]{0,1:T(8,128)S(1)}, f32[512,512]{0,1:T(8,128)}, u32[]{:S(2)}, u32[]{:S(2)}) %collective-permute-start.7) | collective-permute-done | bytes 1048608 | tf_op jit(solution)/shard_map/ppermute | solution.py:74
  888.5 39.3 %custom-call.38 = f32[4,128,128]{1,2,0:T(8,128)S(1)} custom-call(f32[4,128,128]{2,1,0:T(8,128)S(1)} %get-tuple-element.140), custom_call_target="InvertDiagBlocksLowerTriangular" | custom-call | tf_op jit(solution)/shard_map/jit(_solve_triangular)/triangular_solve | solution.py:79
  943.5 85.4 %all-reduce.6.cloned.1.call-done = f32[2048,512]{1,0:T(8,128)} async-done(((f32[2048,512]{1,0:T(8,128)}), f32[2048,512]{1,0:T(8,128)}) %all-reduce.6.cloned.1.call-update) | async-done | bytes 4194320 | tf_op jit(solution)/shard_map/psum | solution.py:13
  1034.1 90.5 %collective-permute-done.8 = f32[2,512,512]{2,1,0:T(8,128)S(1)} collective-permute-done((f32[2,512,512]{2,1,0:T(8,128)S(1)}, f32[2,512,512]{2,1,0:T(8,128)S(1)}, u32[]{:S(2)}, u32[]{:S(2)}) %collective-permute-start.8) | collective-permute-done | bytes 2097184 | tf_op jit(solution)/shard_map/ppermute | solution.py:23
  1125.9 23.7 %collective-permute-done.9 = f32[1,512,512]{2,1,0:T(8,128)S(1)} collective-permute-done((f32[1,512,512]{2,1,0:T(8,128)S(1)}, f32[1,512,512]{2,1,0:T(8,128)S(1)}, u32[]{:S(2)}, u32[]{:S(2)}) %collective-permute-start.9) | collective-permute-done | bytes 1048608 | tf_op jit(solution)/shard_map/ppermute | solution.py:23
  1158.8 118.1 %all-gather.7.cloned.1.call-done = f32[1,4096,512]{2,1,0:T(8,128)} async-done(((f32[1,512,512]{2,1,0:T(8,128)}), f32[1,4096,512]{2,1,0:T(8,128)}) %all-gather.7.cloned.1.call-update) | async-done | bytes 8388624 | tf_op jit(solution)/shard_map/all_gather | solution.py:106
  1281.5 60.9 %subtract_select_fusion = f32[2048,4096]{1,0:T(8,128)} fusion(f32[2048,4096]{1,0:T(8,128)} %fusion.1, pred[4096]{0:T(1024)(128)(4,1)S(1)} %broadcast_compare_fusion, pred[2048]{0:T(1024)(128)(4,1)S(1)} %compare_and_fusion.1, f32[2048,512]{1,0:T(8,128)S(1)} %copy-done.1, f32[4096,512]{1,0:T(8,128)S(1)} %bitcast.178), kind=kOutput, calls=%fused_computation.6 | convolution fusion | flops 51564773376 | bytes 79697920 | tf_op jit(solution)/shard_map/dot_general | solution.py:32
  1344.9 23.6 %collective-permute-done.10 = f32[512,512]{0,1:T(8,128)S(1)} collective-permute-done((f32[512,512]{0,1:T(8,128)S(1)}, f32[512,512]{0,1:T(8,128)S(1)}, u32[]{:S(2)}, u32[]{:S(2)}) %collective-permute-start.10) | collective-permute-done | bytes 1048608 | tf_op jit(solution)/shard_map/ppermute | solution.py:74
  1368.9 23.3 %collective-permute-done.11 = f32[512,512]{0,1:T(8,128)S(1)} collective-permute-done((f32[512,512]{0,1:T(8,128)S(1)}, f32[512,512]{0,1:T(8,128)S(1)}, u32[]{:S(2)}, u32[]{:S(2)}) %collective-permute-start.11) | collective-permute-done | bytes 1048608 | tf_op jit(solution)/shard_map/ppermute | solution.py:74
  1394.3 44.0 %collective-permute-done.12 = f32[512,512]{0,1:T(8,128)S(1)} collective-permute-done((f32[512,512]{0,1:T(8,128)S(1)}, f32[512,512]{0,1:T(8,128)S(1)}, u32[]{:S(2)}, u32[]{:S(2)}) %collective-permute-start.12) | collective-permute-done | bytes 1048608 | tf_op jit(solution)/shard_map/ppermute | solution.py:74
  1464.4 12.2 cholesky.537
  1537.5 39.3 %custom-call.42 = f32[4,128,128]{1,2,0:T(8,128)S(1)} custom-call(f32[4,128,128]{2,1,0:T(8,128)S(1)} %get-tuple-element.141), custom_call_target="InvertDiagBlocksLowerTriangular" | custom-call | tf_op jit(solution)/shard_map/jit(_solve_triangular)/triangular_solve | solution.py:79
  (238 shorter events, 423.4 us)
Async XLA Ops:
  6.5 364.2 %all-reduce.4.cloned.1.call-start = ((), (), s32[]{:S(2)}) async-start(), calls=%async_computation | async-start | bytes 8388608 | tf_op jit(solution)/shard_map/psum | solution.py:13
  31.5 26.2 %collective-permute-start = (f32[512,512]{0,1:T(8,128)S(1)}, f32[512,512]{0,1:T(8,128)S(1)}, u32[]{:S(2)}, u32[]{:S(2)}) collective-permute-start(f32[512,512]{0,1:T(8,128)S(1)} %multiply_multiply_fusion.2), channel_id=1, source_target_pairs={{0,4},{4,0},{8,12},{12,8},{16,20},{20,16},{24,28},{28,24},{1,5},{5... | collective-permute-start | bytes 3145736 | tf_op jit(solution)/shard_map/ppermute | solution.py:74
  58.0 24.4 %collective-permute-start.1 = (f32[512,512]{0,1:T(8,128)S(1)}, f32[512,512]{0,1:T(8,128)S(1)}, u32[]{:S(2)}, u32[]{:S(2)}) collective-permute-start(f32[512,512]{0,1:T(8,128)S(1)} %fusion.186), channel_id=1, source_target_pairs={{0,8},{4,12},{8,0},{12,4},{16,24},{20,28},{24,16},{28,20},{1,9},{5... | collective-permute-start | bytes 3145736 | tf_op jit(solution)/shard_map/ppermute | solution.py:74
  82.6 47.0 %collective-permute-start.2 = (f32[512,512]{0,1:T(8,128)S(1)}, f32[512,512]{0,1:T(8,128)}, u32[]{:S(2)}, u32[]{:S(2)}) collective-permute-start(f32[512,512]{0,1:T(8,128)S(1)} %add.225), channel_id=1, source_target_pairs={{0,16},{4,20},{8,24},{12,28},{16,0},{20,4},{24,8},{28,12},{1,17},{... | collective-permute-start | bytes 3145736 | tf_op jit(solution)/shard_map/ppermute | solution.py:74
  131.6 1.0 copy-start.2
  284.3 342.1 %all-gather.5.cloned.1.call-start = ((), (), s32[]{:S(2)}) async-start(), calls=%async_computation.2 | async-start | bytes 9437184 | tf_op jit(solution)/shard_map/all_gather | solution.py:106
  375.5 93.1 %collective-permute-start.3 = (f32[2,512,512]{2,1,0:T(8,128)}, f32[2,512,512]{2,1,0:T(8,128)S(1)}, u32[]{:S(2)}, u32[]{:S(2)}) collective-permute-start(f32[2,512,512]{2,1,0:T(8,128)} %bitcast.13), channel_id=1, source_target_pairs={{0,16},{16,0},{4,20},{20,4},{8,24},{24,8},{12,28},{28,12},{1,17},{... | collective-permute-start | bytes 6291464 | tf_op jit(solution)/shard_map/ppermute | solution.py:23
  468.6 1.3 copy-start.7
  473.3 24.5 %collective-permute-start.4 = (f32[1,512,512]{2,1,0:T(8,128)}, f32[1,512,512]{2,1,0:T(8,128)}, u32[]{:S(2)}, u32[]{:S(2)}) collective-permute-start(f32[1,512,512]{2,1,0:T(8,128)} %slice_select_fusion.5), channel_id=1, source_target_pairs={{0,8},{8,0},{4,12},{12,4},{16,24},{24,16},{20,28},{28,20},{1,9},{9... | collective-permute-start | bytes 3145736 | tf_op jit(solution)/shard_map/ppermute | solution.py:23
  499.1 529.7 %all-reduce.6.cloned.1.call-start = ((), (), s32[]{:S(2)}) async-start(), calls=%async_computation.1 | async-start | bytes 8388608 | tf_op jit(solution)/shard_map/psum | solution.py:13
  626.3 4.6 copy-start
  693.7 24.2 %collective-permute-start.5 = (f32[512,512]{0,1:T(8,128)S(1)}, f32[512,512]{0,1:T(8,128)S(1)}, u32[]{:S(2)}, u32[]{:S(2)}) collective-permute-start(f32[512,512]{0,1:T(8,128)S(1)} %multiply_multiply_fusion.1), channel_id=1, source_target_pairs={{0,4},{4,0},{8,12},{12,8},{16,20},{20,16},{24,28},{28,24},{1,5},{5... | collective-permute-start | bytes 3145736 | tf_op jit(solution)/shard_map/ppermute | solution.py:74
  718.2 23.4 %collective-permute-start.6 = (f32[512,512]{0,1:T(8,128)S(1)}, f32[512,512]{0,1:T(8,128)S(1)}, u32[]{:S(2)}, u32[]{:S(2)}) collective-permute-start(f32[512,512]{0,1:T(8,128)S(1)} %fusion.185), channel_id=1, source_target_pairs={{0,8},{4,12},{8,0},{12,4},{16,24},{20,28},{24,16},{28,20},{1,9},{5... | collective-permute-start | bytes 3145736 | tf_op jit(solution)/shard_map/ppermute | solution.py:74
  741.8 46.0 %collective-permute-start.7 = (f32[512,512]{0,1:T(8,128)S(1)}, f32[512,512]{0,1:T(8,128)}, u32[]{:S(2)}, u32[]{:S(2)}) collective-permute-start(f32[512,512]{0,1:T(8,128)S(1)} %add.229), channel_id=1, source_target_pairs={{0,16},{4,20},{8,24},{12,28},{16,0},{20,4},{24,8},{28,12},{1,17},{... | collective-permute-start | bytes 3145736 | tf_op jit(solution)/shard_map/ppermute | solution.py:74
  789.8 1.0 copy-start.3
  943.4 333.5 %all-gather.7.cloned.1.call-start = ((), (), s32[]{:S(2)}) async-start(), calls=%async_computation.3 | async-start | bytes 9437184 | tf_op jit(solution)/shard_map/all_gather | solution.py:106
  1031.6 93.0 %collective-permute-start.8 = (f32[2,512,512]{2,1,0:T(8,128)S(1)}, f32[2,512,512]{2,1,0:T(8,128)S(1)}, u32[]{:S(2)}, u32[]{:S(2)}) collective-permute-start(f32[2,512,512]{2,1,0:T(8,128)S(1)} %bitcast.192), channel_id=1, source_target_pairs={{0,16},{16,0},{4,20},{20,4},{8,24},{24,8},{12,28},{28,12},{1,17},{... | collective-permute-start | bytes 6291464 | tf_op jit(solution)/shard_map/ppermute | solution.py:23
  1125.1 25.9 %copy-start.5 = (f32[512,512]{1,0:T(8,128)S(1)}, f32[512,512]{1,0:T(8,128)}, u32[]{:S(2)}) copy-start(f32[512,512]{1,0:T(8,128)} %get-tuple-element.169) | copy-start | bytes 3145732
  1125.3 24.2 %collective-permute-start.9 = (f32[1,512,512]{2,1,0:T(8,128)S(1)}, f32[1,512,512]{2,1,0:T(8,128)S(1)}, u32[]{:S(2)}, u32[]{:S(2)}) collective-permute-start(f32[1,512,512]{2,1,0:T(8,128)S(1)} %slice_select_fusion.4), channel_id=1, source_target_pairs={{0,8},{8,0},{4,12},{12,4},{16,24},{24,16},{20,28},{28,20},{1,9},{9... | collective-permute-start | bytes 3145736 | tf_op jit(solution)/shard_map/ppermute | solution.py:23
  1276.9 4.6 copy-start.1
  1344.3 24.3 %collective-permute-start.10 = (f32[512,512]{0,1:T(8,128)S(1)}, f32[512,512]{0,1:T(8,128)S(1)}, u32[]{:S(2)}, u32[]{:S(2)}) collective-permute-start(f32[512,512]{0,1:T(8,128)S(1)} %multiply_multiply_fusion), channel_id=1, source_target_pairs={{0,4},{4,0},{8,12},{12,8},{16,20},{20,16},{24,28},{28,24},{1,5},{5... | collective-permute-start | bytes 3145736 | tf_op jit(solution)/shard_map/ppermute | solution.py:74
  1368.8 23.4 %collective-permute-start.11 = (f32[512,512]{0,1:T(8,128)S(1)}, f32[512,512]{0,1:T(8,128)S(1)}, u32[]{:S(2)}, u32[]{:S(2)}) collective-permute-start(f32[512,512]{0,1:T(8,128)S(1)} %fusion.184), channel_id=1, source_target_pairs={{0,8},{4,12},{8,0},{12,4},{16,24},{20,28},{24,16},{28,20},{1,9},{5... | collective-permute-start | bytes 3145736 | tf_op jit(solution)/shard_map/ppermute | solution.py:74
  1392.4 45.9 %collective-permute-start.12 = (f32[512,512]{0,1:T(8,128)S(1)}, f32[512,512]{0,1:T(8,128)S(1)}, u32[]{:S(2)}, u32[]{:S(2)}) collective-permute-start(f32[512,512]{0,1:T(8,128)S(1)} %add.232), channel_id=1, source_target_pairs={{0,16},{4,20},{8,24},{12,28},{16,0},{20,4},{24,8},{28,12},{1,17},{... | collective-permute-start | bytes 3145736 | tf_op jit(solution)/shard_map/ppermute | solution.py:74
  1581.6 8.7 copy-start.6
  (1 other events, 1.0 us)
Sparse Core Ops, SparseCore 0:
  284.4 86.2 all-reduce.3
  499.3 127.0 all-gather.4
  943.6 85.2 all-reduce.5
  1151.1 125.8 all-gather.6
